TPU v7x, 32 devices: a whole 2x2x4 slice. The times are simulated.
32 devices in a mesh: az: 8 (over z, y), ax: 4 (over x, core).
Axes of the slice: x: 2, y: 2, z: 4, core: 2. Of those that a mesh axis runs over, the one named last changes fastest.
Arguments:
- acoustic: float32 [4, 64, 64, 128], P(None, 'az', 'ax'), may hold values from -6 to 6
- mean_flow: float32 [4, 64, 64, 128], P(None, 'az', 'ax'), may hold values from -0.4 to 2, as said below
- adjoint_in: float32 [4, 64, 64, 128], P(None, 'az', 'ax'), may hold values from -6 to 6
- admittance: float32 [64], replicated, may hold values from 0.2 to 2
- segment_id: int32 [64, 64], P('az', 'ax'), may hold values from 0 to 63, as said below
- noise_code: int32 [64, 64], P('az', 'ax'), may hold values from 0 to 63
- noise_table: float32 [64], replicated, may hold values from -4 to 4
- mic_az: int32 [512], replicated, may hold values from 0 to 63, as said below
- mic_ax: int32 [512], replicated, may hold values from 0 to 63
- measured: float32 [512], replicated, may hold values from -17 to 17
Outputs:
- adjoint_out: float32 [4, 64, 64, 128], P(None, 'az', 'ax')
- liner_grad: float32 [64], replicated
- misfit: float32 [], replicated
Inputs may be any that keep to these rules, and one draw needn't show every extreme that they name: `mean_flow`: component 0 lies in 0.2 to 0.6, component 1 in -0.4 to 0.4, component 2 in 0.5 to 2, component 3 in 0.7 to 1.4. segment_id = sector * 4 + band, where the 16 sectors are runs of contiguous azimuthal cells (wrapping) and the 4 bands runs of contiguous axial cells; every segment has cells. `mic_az`: microphones sit on casing cells; several may share a cell.
All inputs are finite; a program needn't handle non-finite values.
Results may differ from a plain program's by a relative error of at most 0.000086.
Values sent between devices are 32-bit elements; how exact they have to be, the bound alone decides.
No kernel may reach another device: no remote copies, remote signals or barrier semaphores. Data moves between devices by JAX's collectives and lax.ppermute only.
A program may use at most 128 MiB of HBM per device.

v0:
```python
import jax
import jax.numpy as jnp
from jax import lax
from jax.sharding import PartitionSpec as P

step_dt = 0.25
epsilon = 1e-06
highest = lax.Precision.HIGHEST


def with_halo(array, sides, width, wrap):
    for axis, dim in sides:
        size, length = (lax.axis_size(axis), array.shape[dim])
        up = [(i, (i + 1) % size) for i in range(size if wrap else size - 1)]
        down = [(j, i) for i, j in up]
        last = lax.slice_in_dim(array, length - width, length, axis=dim)
        initial = lax.slice_in_dim(array, 0, width, axis=dim)
        before = lax.ppermute(last, axis, up)
        after = lax.ppermute(initial, axis, down)
        array = jnp.concatenate([before, array, after], axis=dim)
    return array


def center(values):
    return values[..., 1:-1, 1:-1, :]


def az_next(values):
    return values[..., 2:, 1:-1, :]


def az_prev(values):
    return values[..., :-2, 1:-1, :]


def ax_next(values):
    return values[..., 1:-1, 2:, :]


def ax_prev(values):
    return values[..., 1:-1, :-2, :]


def shrink(values, margin):
    return values[..., margin : values.shape[-3] - margin, margin : values.shape[-2] - margin, :]


def rad_next(values):
    return jnp.concatenate([values[..., 1:], jnp.zeros_like(values[..., :1])], axis=-1)


def rad_prev(values):
    return jnp.concatenate([jnp.zeros_like(values[..., :1]), values[..., :-1]], axis=-1)


def casing_mask(values):
    return lax.broadcasted_iota(jnp.int32, values.shape, values.ndim - 1) == values.shape[-1] - 1


def advect(values, axial_flow, swirl_flow):
    return (
        center(axial_flow) * (ax_next(values) - ax_prev(values)) * 0.5
        + center(swirl_flow) * (az_next(values) - az_prev(values)) * 0.5
    )


def advect_back(values, axial_flow, swirl_flow):
    carried_ax = axial_flow * values
    carried_az = swirl_flow * values
    return 0.5 * (ax_prev(carried_ax) - ax_next(carried_ax)) + 0.5 * (
        az_prev(carried_az) - az_next(carried_az)
    )


def exchange_rims(fields, rim_width):
    widened = with_halo(fields, (("ax", 2),), rim_width, False)
    return with_halo(widened, (("az", 1),), rim_width, True)


def forward_pressure(padded, wall_admit, source):
    pressure, vel_az, vel_ax, vel_rad = (padded[0], padded[1], padded[2], padded[3])
    axial_flow, swirl_flow, buoyancy, stiffness = (padded[4], padded[5], padded[6], padded[7])
    new_az = center(vel_az) - step_dt * (
        advect(vel_az, axial_flow, swirl_flow)
        + center(buoyancy) * (az_next(pressure) - center(pressure))
    )
    new_ax = center(vel_ax) - step_dt * (
        advect(vel_ax, axial_flow, swirl_flow)
        + center(buoyancy) * (ax_next(pressure) - center(pressure))
    )
    press_in = shrink(pressure, 1)
    rad_in = shrink(vel_rad, 1)
    axial_in = shrink(axial_flow, 1)
    swirl_in = shrink(swirl_flow, 1)
    buoy_in = shrink(buoyancy, 1)
    stiff_in = shrink(stiffness, 1)
    press_own = center(press_in)
    new_rad = jnp.where(
        casing_mask(press_own),
        wall_admit[:, :, None] * press_own,
        center(rad_in)
        - step_dt
        * (
            advect(rad_in, axial_in, swirl_in) + center(buoy_in) * (rad_next(press_own) - press_own)
        ),
    )
    spread = (
        center(new_az)
        - az_prev(new_az)
        + (center(new_ax) - ax_prev(new_ax))
        + (new_rad - rad_prev(new_rad))
    )
    return (
        press_own
        - step_dt * (advect(press_in, axial_in, swirl_in) + center(stiff_in) * spread)
        + step_dt * source
    )


def first_half(press_pad, vel_pad, coef_pad):
    pushed = step_dt * coef_pad[3] * press_pad
    pushed_own = center(pushed)
    head_az = vel_pad[0] - (pushed_own - az_next(pushed))
    head_ax = vel_pad[1] - (pushed_own - ax_next(pushed))
    head_rad = vel_pad[2] - (pushed_own - rad_next(pushed_own))
    return jnp.stack([head_az, head_ax, head_rad])


def second_half(press_pad, head_stack, coef_pad, wall_admit):
    axial_flow, swirl_flow, buoyancy = (coef_pad[0], coef_pad[1], coef_pad[2])
    head_az, head_ax = (head_stack[0], head_stack[1])
    head_masked = jnp.where(casing_mask(head_stack[2]), 0.0, head_stack[2])
    back_az = center(head_az) - step_dt * advect_back(head_az, axial_flow, swirl_flow)
    back_ax = center(head_ax) - step_dt * advect_back(head_ax, axial_flow, swirl_flow)
    back_rad = center(head_masked) - step_dt * advect_back(head_masked, axial_flow, swirl_flow)
    push_az = step_dt * buoyancy * head_az
    push_ax = step_dt * buoyancy * head_ax
    push_rad = step_dt * center(buoyancy) * center(head_masked)
    rad_own = center(head_stack[2])
    back_press = center(press_pad) - step_dt * advect_back(press_pad, axial_flow, swirl_flow)
    back_press = (
        back_press
        + (center(push_az) - az_prev(push_az))
        + (center(push_ax) - ax_prev(push_ax))
        + (push_rad - rad_prev(push_rad))
    )
    back_press = back_press + jnp.where(casing_mask(rad_own), wall_admit[:, :, None] * rad_own, 0.0)
    return (jnp.stack([back_press, back_az, back_ax, back_rad]), rad_own[..., -1])


def adjoint_step(seed_list, velocity_list, coef_wide, wall_admit, rim_width):
    joined = exchange_rims(jnp.stack(seed_list), rim_width)
    coef_first = shrink(coef_wide, 2 - rim_width)
    coef_second = shrink(coef_wide, 1)
    member = 0
    head_list = first_half(joined[member], velocity_list[member], coef_first)
    widened = exchange_rims(head_list, 1)
    member = 0
    results = [second_half(joined[member], widened, coef_second, wall_admit)]
    return results


def shards(
    acoustic,
    mean_flow,
    adjoint_in,
    admittance,
    segment_id,
    noise_code,
    noise_table,
    mic_az,
    mic_ax,
    measured,
):
    az_cells, ax_cells, rad_cells = (acoustic.shape[1], acoustic.shape[2], acoustic.shape[3])
    buoyancy = 1.0 / mean_flow[2]
    stiffness = mean_flow[2] * mean_flow[3] * mean_flow[3]
    segment_hot = (
        segment_id[:, :, None] == lax.broadcasted_iota(jnp.int32, (1, 1, admittance.shape[0]), 2)
    ).astype(jnp.float32)
    wall_admit = jnp.dot(segment_hot, admittance, precision=highest)
    noise_hot = (
        noise_code[:, :, None] == lax.broadcasted_iota(jnp.int32, (1, 1, noise_table.shape[0]), 2)
    ).astype(jnp.float32)
    profile = (lax.broadcasted_iota(jnp.float32, (rad_cells,), 0) + 0.5) / rad_cells
    source = jnp.dot(noise_hot, noise_table, precision=highest)[:, :, None] * profile
    coefficients = jnp.stack([mean_flow[0], mean_flow[1], buoyancy, stiffness])
    rim_width = 1
    padded = exchange_rims(jnp.concatenate([acoustic, coefficients], axis=0), 2)
    velocities = adjoint_in[1:]
    coef_wide = padded[4:8]
    new_press = forward_pressure(padded, wall_admit, source)
    first_az = lax.axis_index("az") * az_cells
    first_ax = lax.axis_index("ax") * ax_cells
    local_az = mic_az - first_az
    local_ax = mic_ax - first_ax
    owned = (local_az >= 0) & (local_az < az_cells) & (local_ax >= 0) & (local_ax < ax_cells)
    flat_cell = jnp.clip(local_az, 0, az_cells - 1) * ax_cells + jnp.clip(local_ax, 0, ax_cells - 1)
    heard = new_press[:, :, rad_cells - 1].reshape(az_cells * ax_cells)[flat_cell]
    misses = jnp.where(owned, heard - measured, 0.0)
    square_sum = jnp.sum(misses * misses)
    mic_count = mic_az.shape[0]
    casing_own = acoustic[0][:, :, rad_cells - 1]
    grad_scale = (
        az_cells * lax.axis_size("az") * ax_cells * lax.axis_size("ax") / admittance.shape[0]
    ) ** (-0.5)
    total_sq = lax.psum(square_sum, ("az", "ax"))
    mean_sq = total_sq / mic_count + epsilon
    placed = (
        jnp.zeros((az_cells * ax_cells,), jnp.float32)
        .at[flat_cell]
        .add(jnp.where(owned, misses / mean_sq, 0.0))
        .reshape(az_cells, ax_cells)
    )
    seed_press = adjoint_in[0] + jnp.where(casing_mask(adjoint_in[0]), placed[:, :, None], 0.0)
    outcome = adjoint_step([seed_press], [velocities], coef_wide, wall_admit, rim_width)
    adjoint_out, rad_top = outcome[0]
    segment_sums = jnp.einsum("acs,ac->s", segment_hot, rad_top * casing_own, precision=highest)
    liner_grad = lax.psum(segment_sums, ("az", "ax")) * grad_scale
    misfit = 0.5 * jnp.log(mean_sq)
    return (adjoint_out, liner_grad, misfit)


def solution(mesh):
    placed = (
        P(None, "az", "ax", None),
        P(None, "az", "ax", None),
        P(None, "az", "ax", None),
        P(),
        P("az", "ax"),
        P("az", "ax"),
        P(),
        P(),
        P(),
        P(),
    )
    return jax.shard_map(
        shards,
        mesh=mesh,
        in_specs=placed,
        out_specs=(P(None, "az", "ax", None), P(), P()),
        check_vma=False,
    )
```

profile of v0, /device:TPU:14, one launch (start us, length us, event | category | flops | bytes accessed | tf_op | source)
XLA Modules:
  0.0 222.4 jit_solution(4559688916384890473)
XLA Ops:
  0.6 0.9 slice_divide_fusion
  1.5 0.9 slice.363
  2.5 1.0 pad_maximum_fusion.6
  3.7 1.9 collective-permute-start.1
  5.6 2.4 %collective-permute-start = (f32[8,8,2,128]{3,1,2,0:T(8,128)S(1)}, f32[8,8,2,128]{3,1,2,0:T(8,128)S(1)}, u32[]{:S(2)}, u32[]{:S(2)}) collective-permute-start(f32[8,8,2,128]{3,1,2,0:T(8,128)S(1)} %copy.107), channel_id=1, source_target_pairs={{0,1},{1,2},{2,3},{4,5},{5,6},{6,7},{8,9},{9,10},{10,11},{12,13},{... | collective-permute-start | bytes 196616 | tf_op jit(solution)/shard_map/ppermute | solution.py:18
  8.0 2.7 %copy.81 = f32[8,8,16,128]{2,1,3,0:T(8,128)} copy(f32[8,8,16,128]{3,2,1,0:T(8,128)S(1)} %pad_maximum_fusion.6) | data formatting | bytes 1048576 | tf_op jit(solution)/shard_map/concatenate | solution.py:189
  11.6 2.7 %copy.82 = f32[8,8,2,128]{2,1,3,0:T(8,128)} copy(f32[8,8,2,128]{3,1,2,0:T(8,128)S(1)} %collective-permute-done.1) | data formatting | bytes 131072 | tf_op jit(solution)/shard_map/ppermute | solution.py:19
  14.3 2.7 %copy.80 = f32[8,8,2,128]{2,1,3,0:T(8,128)} copy(f32[8,8,2,128]{3,1,2,0:T(8,128)S(1)} %collective-permute-done) | data formatting | bytes 131072 | tf_op jit(solution)/shard_map/ppermute | solution.py:18
  17.0 12.7 %pad_maximum_fusion.5 = (f32[8,2,20,128]{2,1,3,0:T(2,128)S(1)}, f32[8,2,20,128]{2,1,3,0:T(2,128)S(1)}) fusion(f32[8,8,2,128]{2,1,3,0:T(8,128)} %copy.82, f32[8,8,16,128]{2,1,3,0:T(8,128)} %copy.81, f32[8,8,2,128]{2,1,3,0:T(8,128)} %copy.80), kind=kLoop, calls=%fused_computation.47 | loop fusion | flops 163840 | bytes 983040 | tf_op jit(solution)/shard_map/slice | solution.py:16
  31.0 2.6 %collective-permute-start.2 = (f32[8,2,20,128]{3,0,2,1:T(8,128)S(1)}, f32[8,2,20,128]{3,0,2,1:T(8,128)S(1)}, u32[]{:S(2)}, u32[]{:S(2)}) collective-permute-start(f32[8,2,20,128]{3,0,2,1:T(8,128)S(1)} %copy.83), channel_id=1, source_target_pairs={{0,4},{4,8},{8,12},{12,16},{16,20},{20,24},{24,28},{28,0},{1,5},{5... | collective-permute-start | bytes 491528 | tf_op jit(solution)/shard_map/ppermute | solution.py:18
  34.2 2.9 %collective-permute-done.3 = f32[8,2,20,128]{3,0,2,1:T(8,128)S(1)} collective-permute-done((f32[8,2,20,128]{3,0,2,1:T(8,128)S(1)}, f32[8,2,20,128]{3,0,2,1:T(8,128)S(1)}, u32[]{:S(2)}, u32[]{:S(2)}) %collective-permute-start.3) | collective-permute-done | bytes 163872 | tf_op jit(solution)/shard_map/ppermute | solution.py:19
  37.6 2.3 %collective-permute-done.2 = f32[8,2,20,128]{3,0,2,1:T(8,128)S(1)} collective-permute-done((f32[8,2,20,128]{3,0,2,1:T(8,128)S(1)}, f32[8,2,20,128]{3,0,2,1:T(8,128)S(1)}, u32[]{:S(2)}, u32[]{:S(2)}) %collective-permute-start.2) | collective-permute-done | bytes 163872 | tf_op jit(solution)/shard_map/ppermute | solution.py:18
  40.4 7.7 %pad_maximum_fusion = f32[8,12,20,128]{2,1,3,0:T(8,128)S(1)} fusion(f32[8,2,20,128]{2,1,3,0:T(2,128)S(1)} %copy.86, f32[8,8,2,128]{2,1,3,0:T(8,128)} %copy.82, f32[8,8,16,128]{2,1,3,0:T(8,128)} %copy.81, f32[8,8,2,128]{2,1,3,0:T(8,128)} %copy.80, f32[8,2,20,128]{2,1,3,0:T(2,128)S(1)} %copy.85), kind=kLoop, calls=%fused_computation.2 | loop fusion | flops 983040 | bytes 1966080 | tf_op jit(solution)/shard_map/concatenate | solution.py:20
  48.7 2.7 %copy-done.2 = f32[8,12,20,128]{2,1,3,0:T(8,128)} copy-done((f32[8,12,20,128]{2,1,3,0:T(8,128)}, f32[8,12,20,128]{2,1,3,0:T(8,128)S(1)}, u32[]{:S(2)}) %copy-start.2) | copy-done | bytes 983064
  51.8 2.5 %fusion.5 = f32[10,18,128]{1,0,2:T(8,128)S(1)} fusion(f32[12,20,128]{1,0,2:T(8,128)S(1)} %get-tuple-element.33, f32[12,20,128]{1,0,2:T(8,128)S(1)} %get-tuple-element.28, f32[12,20,128]{1,0,2:T(8,128)S(1)} %get-tuple-element.29, f32[12,20,128]{1,0,2:T(8,128)S(1)} %get-tuple-element.31, f32[12,20,128]{1,0,2:T(8,128)S(1)} %get-tuple-element.32), kind=kLoop, calls=%fused_computation.20 | loop fusion | flops 253440 | bytes 1013760 | tf_op jit(solution)/shard_map/sub | solution.py:87
  54.3 2.5 %fusion.13 = f32[10,18,128]{1,0,2:T(8,128)S(1)} fusion(f32[12,20,128]{1,0,2:T(8,128)S(1)} %get-tuple-element.33, f32[12,20,128]{1,0,2:T(8,128)S(1)} %get-tuple-element.26, f32[12,20,128]{1,0,2:T(8,128)S(1)} %get-tuple-element.29, f32[12,20,128]{1,0,2:T(8,128)S(1)} %get-tuple-element.31, f32[12,20,128]{1,0,2:T(8,128)S(1)} %get-tuple-element.32), kind=kLoop, calls=%fused_computation.32 | loop fusion | flops 253440 | bytes 1013760 | tf_op jit(solution)/shard_map/sub | solution.py:83
  56.8 2.0 fusion.62
  60.0 3.3 %gather_fusion = f32[512]{0:T(512)S(1)} fusion(f32[128]{0:T(128)S(1)} %reshape_squeeze.3, s32[1024]{0:T(1024)S(1)} %pad_clamp_fusion), kind=kCustom, calls=%fused_computation | custom fusion | bytes 6144 | tf_op jit(solution)/shard_map/gather | solution.py:199
  64.0 43.0 %psum.14 = f32[]{:T(128)} all-reduce(f32[]{:T(128)} %get-tuple-element.11), channel_id=1, replica_groups=mesh['az'=8,'ax'=4] {'az','ax'}, use_global_device_ids=true, to_apply=%region_1.2 | all-reduce | flops 1 | bytes 8 | tf_op jit(solution)/shard_map/psum | solution.py:207
  107.7 4.1 %scatter_custom_fusion = f32[128]{0:T(128)S(1)} fusion(s32[512]{0:T(512)S(1)} %compare_select_fusion, f32[512]{0:T(512)S(1)} %divide_select_fusion, f32[]{:T(128)} %constant.19.clone.1), kind=kCustom, calls=%fused_computation.159 | custom fusion | flops 512 | bytes 516 | tf_op jit(solution)/shard_map/scatter-add | solution.py:212
  112.1 1.9 collective-permute-start.5
  114.0 2.4 %collective-permute-start.4 = (f32[1,8,1,128]{3,1,2,0:T(8,128)S(1)}, f32[1,8,1,128]{3,1,2,0:T(8,128)S(1)}, u32[]{:S(2)}, u32[]{:S(2)}) collective-permute-start(f32[1,8,1,128]{3,1,2,0:T(8,128)S(1)} %get-tuple-element.60), channel_id=1, source_target_pairs={{0,1},{1,2},{2,3},{4,5},{5,6},{6,7},{8,9},{9,10},{10,11},{12,13},{... | collective-permute-start | bytes 12296 | tf_op jit(solution)/shard_map/ppermute | solution.py:18
  116.4 2.9 %collective-permute-done.4 = f32[1,8,1,128]{3,1,2,0:T(8,128)S(1)} collective-permute-done((f32[1,8,1,128]{3,1,2,0:T(8,128)S(1)}, f32[1,8,1,128]{3,1,2,0:T(8,128)S(1)}, u32[]{:S(2)}, u32[]{:S(2)}) %collective-permute-start.4) | collective-permute-done | bytes 4128 | tf_op jit(solution)/shard_map/ppermute | solution.py:18
  119.4 1.5 collective-permute-start.7
  121.0 1.5 collective-permute-start.6
  123.3 1.0 copy.112
  124.6 0.7 collective-permute-done.6
  125.3 4.2 %fusion.21 = (f32[10,18,128]{1,0,2:T(8,128)}, f32[10,18,128]{1,0,2:T(8,128)S(1)}, f32[10,18,128]{1,0,2:T(8,128)}) fusion(f32[8,12,20,128]{2,1,3,0:T(8,128)} %copy-done.2, f32[1,1,18,128]{2,1,3,0:T(1,128)S(1)} %collective-permute-done.7, f32[1,8,18,128]{2,1,3,0:T(8,128)S(1)} %copy.90, f32[1,1,18,128]{2,1,3,0:T(1,128)S(1)} %collective-permute-done.6), kind=kLoop, calls=%fused_computation.54 | loop fusion | flops 138240 | bytes 645120 | tf_op jit(solution)/shard_map/mul | solution.py:68
  131.8 2.1 collective-permute-start.9
  134.5 2.2 collective-permute-start.8
  136.7 2.6 %slice_bitcast_fusion.3 = f32[10,18,128]{1,0,2:T(8,128)} fusion(f32[8,12,20,128]{2,1,3,0:T(8,128)} %copy-done.2), kind=kLoop, calls=%fused_computation.12 | loop fusion | bytes 184320 | tf_op jit(solution)/shard_map/squeeze | solution.py:130
  140.5 3.8 %pad_maximum_fusion.12 = (f32[3,1,18,128]{2,1,3,0:T(1,128)S(1)}, f32[3,1,18,128]{2,1,3,0:T(1,128)S(1)}) fusion(f32[3,8,1,128]{2,1,3,0:T(8,128)S(1)} %copy.97, f32[3,8,1,128]{2,1,3,0:T(8,128)S(1)} %copy.96, f32[1,8,16,128]{2,1,3,0:T(8,128)} %copy-done.7, f32[1,8,16,128]{2,1,3,0:T(8,128)} %copy-done.5, f32[1,8,16,128]{2,1,3,0:T(8,128)} %copy-done.3), kind=kLoop, calls=%fused_computation.127 | loop fusion | flops 55296 | bytes 276480 | tf_op jit(solution)/shard_map/slice | solution.py:16
  144.3 1.0 collective-permute-start.11
  145.3 2.0 collective-permute-start.10
  147.3 1.2 maximum_bitcast_fusion
  148.5 4.7 %collective-permute-done.11 = f32[3,1,18,128]{2,1,3,0:T(1,128)S(1)} collective-permute-done((f32[3,1,18,128]{2,1,3,0:T(1,128)S(1)}, f32[3,1,18,128]{2,1,3,0:T(1,128)S(1)}, u32[]{:S(2)}, u32[]{:S(2)}) %collective-permute-start.11) | collective-permute-done | bytes 27680 | tf_op jit(solution)/shard_map/ppermute | solution.py:19
  153.2 2.2 collective-permute-done.10
  155.4 1.7 pad_maximum_fusion.1
  157.2 4.9 %multiply_multiply_fusion.1 = (f32[10,18,128]{1,0,2:T(8,128)}, f32[10,18,128]{1,0,2:T(8,128)}, f32[10,18,128]{1,0,2:T(8,128)S(1)}, f32[10,18,128]{1,0,2:T(8,128)...) fusion(f32[8,12,20,128]{2,1,3,0:T(8,128)} %copy-done.2, ...), kind=kLoop, calls=%fused_computation.50 | loop fusion | flops 207360 | bytes 1290368 | tf_op jit(solution)/shard_map/mul | solution.py:136
  162.1 1.8 slice_bitcast_fusion
  163.9 1.7 fusion.22
  165.6 0.7 fusion.41
  166.5 3.1 %fusion.33 = f32[1,8,16,128]{2,1,3,0:T(8,128)S(1)} fusion(f32[10,18,128]{1,0,2:T(8,128)} %get-tuple-element.18, f32[10,18,128]{1,0,2:T(8,128)} %get-tuple-element.20, f32[10,18,128]{1,0,2:T(8,128)} %get-tuple-element.37), kind=kLoop, calls=%fused_computation.69 | loop fusion | flops 81920 | bytes 393216 | tf_op jit(solution)/shard_map/stack | solution.py:148
  169.7 1.9 fusion.37
  171.9 5.0 %fusion.40 = f32[1,8,16,128]{2,1,3,0:T(8,128)S(1)} fusion(f32[10,18,128]{1,0,2:T(8,128)} %get-tuple-element.36, f32[10,18,128]{1,0,2:T(8,128)} %get-tuple-element.16, f32[10,18,128]{1,0,2:T(8,128)} %get-tuple-element.15, f32[10,18,128]{1,0,2:T(8,128)} %get-tuple-element.25, f32[10,18,128]{1,0,2:T(8,128)} %get-tuple-element.23, ...), kind=kLoop, calls=%fused_computation.80 | loop fusion | flops 229376 | bytes 852096 | tf_op jit(solution)/shard_map/stack | solution.py:148
  177.1 0.8 slice_multiply_fusion.4
  178.1 41.9 %psum.15 = f32[64]{0:T(128)S(1)} all-reduce(f32[64]{0:T(128)S(1)} %convolution_bitcast_fusion), channel_id=1, replica_groups=mesh['az'=8,'ax'=4] {'az','ax'}, use_global_device_ids=true, to_apply=%region_3.4 | all-reduce | flops 64 | bytes 512 | tf_op jit(solution)/shard_map/psum | solution.py:219
  220.5 0.7 pad_maximum_fusion.7
  (97 shorter events, 13.7 us)
Async XLA Ops:
  0.6 10.1 %copy-start = (f32[64]{0:T(128)S(1)}, f32[64]{0:T(128)}, u32[]{:S(2)}) copy-start(f32[64]{0:T(128)} %param.13) | copy-start | bytes 772
  2.5 8.2 %copy-start.12 = (f32[4,8,16,128]{3,2,1,0:T(8,128)S(1)}, f32[4,8,16,128]{3,2,1,0:T(8,128)}, u32[]{:S(2)}) copy-start(f32[4,8,16,128]{3,2,1,0:T(8,128)} %param.12) | copy-start | bytes 786436
  3.5 7.2 %copy-start.17 = (s32[8,16]{1,0:T(8,128)S(1)}, s32[8,16]{1,0:T(8,128)}, u32[]{:S(2)}) copy-start(s32[8,16]{1,0:T(8,128)} %param.14) | copy-start | bytes 1540
  3.5 7.6 %copy-start.16 = (s32[8,16]{1,0:T(8,128)S(1)}, s32[8,16]{1,0:T(8,128)}, u32[]{:S(2)}) copy-start(s32[8,16]{1,0:T(8,128)} %param.15) | copy-start | bytes 1540
  3.5 7.6 %copy-start.18 = (f32[64]{0:T(128)S(1)}, f32[64]{0:T(128)}, u32[]{:S(2)}) copy-start(f32[64]{0:T(128)} %param.16) | copy-start | bytes 772
  3.6 8.0 %copy-start.13 = (s32[512]{0:T(512)S(1)}, s32[512]{0:T(512)}, u32[]{:S(2)}) copy-start(s32[512]{0:T(512)} %param.18) | copy-start | bytes 6148
  3.6 8.0 %copy-start.14 = (s32[512]{0:T(512)S(1)}, s32[512]{0:T(512)}, u32[]{:S(2)}) copy-start(s32[512]{0:T(512)} %param.17) | copy-start | bytes 6148
  3.7 8.0 %collective-permute-start.1 = (f32[8,8,2,128]{3,1,2,0:T(8,128)S(1)}, f32[8,8,2,128]{3,1,2,0:T(8,128)S(1)}, u32[]{:S(2)}, u32[]{:S(2)}) collective-permute-start(f32[8,8,2,128]{3,1,2,0:T(8,128)S(1)} %copy.108), channel_id=1, source_target_pairs={{1,0},{2,1},{3,2},{5,4},{6,5},{7,6},{9,8},{10,9},{11,10},{13,12},{... | collective-permute-start | bytes 196616 | tf_op jit(solution)/shard_map/ppermute | solution.py:19
  5.6 8.7 %collective-permute-start = (f32[8,8,2,128]{3,1,2,0:T(8,128)S(1)}, f32[8,8,2,128]{3,1,2,0:T(8,128)S(1)}, u32[]{:S(2)}, u32[]{:S(2)}) collective-permute-start(f32[8,8,2,128]{3,1,2,0:T(8,128)S(1)} %copy.107), channel_id=1, source_target_pairs={{0,1},{1,2},{2,3},{4,5},{5,6},{6,7},{8,9},{9,10},{10,11},{12,13},{... | collective-permute-start | bytes 196616 | tf_op jit(solution)/shard_map/ppermute | solution.py:18
  30.1 7.1 %collective-permute-start.3 = (f32[8,2,20,128]{3,0,2,1:T(8,128)S(1)}, f32[8,2,20,128]{3,0,2,1:T(8,128)S(1)}, u32[]{:S(2)}, u32[]{:S(2)}) collective-permute-start(f32[8,2,20,128]{3,0,2,1:T(8,128)S(1)} %copy.84), channel_id=1, source_target_pairs={{4,0},{8,4},{12,8},{16,12},{20,16},{24,20},{28,24},{0,28},{5,1},{9... | collective-permute-start | bytes 491528 | tf_op jit(solution)/shard_map/ppermute | solution.py:19
  31.0 9.0 %collective-permute-start.2 = (f32[8,2,20,128]{3,0,2,1:T(8,128)S(1)}, f32[8,2,20,128]{3,0,2,1:T(8,128)S(1)}, u32[]{:S(2)}, u32[]{:S(2)}) collective-permute-start(f32[8,2,20,128]{3,0,2,1:T(8,128)S(1)} %copy.83), channel_id=1, source_target_pairs={{0,4},{4,8},{8,12},{12,16},{16,20},{20,24},{24,28},{28,0},{1,5},{5... | collective-permute-start | bytes 491528 | tf_op jit(solution)/shard_map/ppermute | solution.py:18
  48.1 3.3 %copy-start.2 = (f32[8,12,20,128]{2,1,3,0:T(8,128)}, f32[8,12,20,128]{2,1,3,0:T(8,128)S(1)}, u32[]{:S(2)}) copy-start(f32[8,12,20,128]{2,1,3,0:T(8,128)S(1)} %pad_maximum_fusion) | copy-start | bytes 2949124
  58.8 4.6 %copy-start.15 = (f32[512]{0:T(512)S(1)}, f32[512]{0:T(512)}, u32[]{:S(2)}) copy-start(f32[512]{0:T(512)} %param.19) | copy-start | bytes 6148
  59.3 64.0 %slice-start = ((f32[4,8,16,128]{3,2,1,0:T(8,128)}), f32[1,8,16,128]{3,2,1,0:T(8,128)S(1)}, s32[]{:S(2)}) async-start(f32[4,8,16,128]{3,2,1,0:T(8,128)} %param.10), calls=%async_computation | async-start | bytes 131072 | tf_op jit(solution)/shard_map/slice | solution.py:203
  112.1 4.3 %collective-permute-start.5 = (f32[1,8,1,128]{3,1,2,0:T(8,128)S(1)}, f32[1,8,1,128]{3,1,2,0:T(8,128)S(1)}, u32[]{:S(2)}, u32[]{:S(2)}) collective-permute-start(f32[1,8,1,128]{3,1,2,0:T(8,128)S(1)} %get-tuple-element.61), channel_id=1, source_target_pairs={{1,0},{2,1},{3,2},{5,4},{6,5},{7,6},{9,8},{10,9},{11,10},{13,12},{... | collective-permute-start | bytes 12296 | tf_op jit(solution)/shard_map/ppermute | solution.py:19
  114.0 5.3 %collective-permute-start.4 = (f32[1,8,1,128]{3,1,2,0:T(8,128)S(1)}, f32[1,8,1,128]{3,1,2,0:T(8,128)S(1)}, u32[]{:S(2)}, u32[]{:S(2)}) collective-permute-start(f32[1,8,1,128]{3,1,2,0:T(8,128)S(1)} %get-tuple-element.60), channel_id=1, source_target_pairs={{0,1},{1,2},{2,3},{4,5},{5,6},{6,7},{8,9},{9,10},{10,11},{12,13},{... | collective-permute-start | bytes 12296 | tf_op jit(solution)/shard_map/ppermute | solution.py:18
  119.4 5.2 %collective-permute-start.7 = (f32[1,1,18,128]{2,1,3,0:T(1,128)S(1)}, f32[1,1,18,128]{2,1,3,0:T(1,128)S(1)}, u32[]{:S(2)}, u32[]{:S(2)}) collective-permute-start(f32[1,1,18,128]{2,1,3,0:T(1,128)S(1)} %copy.89), channel_id=1, source_target_pairs={{4,0},{8,4},{12,8},{16,12},{20,16},{24,20},{28,24},{0,28},{5,1},{9... | collective-permute-start | bytes 27656 | tf_op jit(solution)/shard_map/ppermute | solution.py:19
  121.0 4.3 %collective-permute-start.6 = (f32[1,1,18,128]{2,1,3,0:T(1,128)S(1)}, f32[1,1,18,128]{2,1,3,0:T(1,128)S(1)}, u32[]{:S(2)}, u32[]{:S(2)}) collective-permute-start(f32[1,1,18,128]{2,1,3,0:T(1,128)S(1)} %copy.88), channel_id=1, source_target_pairs={{0,4},{4,8},{8,12},{12,16},{16,20},{20,24},{24,28},{28,0},{1,5},{5... | collective-permute-start | bytes 27656 | tf_op jit(solution)/shard_map/ppermute | solution.py:18
  124.5 5.0 %copy-start.9 = (f32[1,8,18,128]{2,1,3,0:T(8,128)}, f32[1,8,18,128]{2,1,3,0:T(8,128)S(1)}, u32[]{:S(2)}) copy-start(f32[1,8,18,128]{2,1,3,0:T(8,128)S(1)} %copy.90) | copy-start | bytes 221188
  130.2 0.8 copy-start.3
  130.2 1.0 copy-start.5
  130.2 1.1 copy-start.7
  131.8 7.5 %collective-permute-start.9 = (f32[3,8,1,128]{3,1,2,0:T(8,128)S(1)}, f32[3,8,1,128]{3,1,2,0:T(8,128)S(1)}, u32[]{:S(2)}, u32[]{:S(2)}) collective-permute-start(f32[3,8,1,128]{3,1,2,0:T(8,128)S(1)} %copy.95), channel_id=1, source_target_pairs={{1,0},{2,1},{3,2},{5,4},{6,5},{7,6},{9,8},{10,9},{11,10},{13,12},{... | collective-permute-start | bytes 36872 | tf_op jit(solution)/shard_map/ppermute | solution.py:19
  134.5 5.4 %collective-permute-start.8 = (f32[3,8,1,128]{3,1,2,0:T(8,128)S(1)}, f32[3,8,1,128]{3,1,2,0:T(8,128)S(1)}, u32[]{:S(2)}, u32[]{:S(2)}) collective-permute-start(f32[3,8,1,128]{3,1,2,0:T(8,128)S(1)} %copy.94), channel_id=1, source_target_pairs={{0,1},{1,2},{2,3},{4,5},{5,6},{6,7},{8,9},{9,10},{10,11},{12,13},{... | collective-permute-start | bytes 36872 | tf_op jit(solution)/shard_map/ppermute | solution.py:18
  140.5 6.8 %copy-start.10 = (f32[1,8,18,128]{2,1,3,0:T(8,128)S(1)}, f32[1,8,18,128]{2,1,3,0:T(8,128)}, u32[]{:S(2)}) copy-start(f32[1,8,18,128]{2,1,3,0:T(8,128)} %copy-done.9) | copy-start | bytes 221188
  140.5 14.9 %copy-start.4 = (f32[1,8,16,128]{2,1,3,0:T(8,128)S(1)}, f32[1,8,16,128]{2,1,3,0:T(8,128)}, u32[]{:S(2)}) copy-start(f32[1,8,16,128]{2,1,3,0:T(8,128)} %copy-done.3) | copy-start | bytes 196612
  140.5 14.9 %copy-start.6 = (f32[1,8,16,128]{2,1,3,0:T(8,128)S(1)}, f32[1,8,16,128]{2,1,3,0:T(8,128)}, u32[]{:S(2)}) copy-start(f32[1,8,16,128]{2,1,3,0:T(8,128)} %copy-done.5) | copy-start | bytes 196612
  140.5 14.9 %copy-start.8 = (f32[1,8,16,128]{2,1,3,0:T(8,128)S(1)}, f32[1,8,16,128]{2,1,3,0:T(8,128)}, u32[]{:S(2)}) copy-start(f32[1,8,16,128]{2,1,3,0:T(8,128)} %copy-done.7) | copy-start | bytes 196612
  144.3 8.9 %collective-permute-start.11 = (f32[3,1,18,128]{2,1,3,0:T(1,128)S(1)}, f32[3,1,18,128]{2,1,3,0:T(1,128)S(1)}, u32[]{:S(2)}, u32[]{:S(2)}) collective-permute-start(f32[3,1,18,128]{2,1,3,0:T(1,128)S(1)} %get-tuple-element.35), channel_id=1, source_target_pairs={{4,0},{8,4},{12,8},{16,12},{20,16},{24,20},{28,24},{0,28},{5,1},{9... | collective-permute-start | bytes 82952 | tf_op jit(solution)/shard_map/ppermute | solution.py:19
  145.3 10.1 %collective-permute-start.10 = (f32[3,1,18,128]{2,1,3,0:T(1,128)S(1)}, f32[3,1,18,128]{2,1,3,0:T(1,128)S(1)}, u32[]{:S(2)}, u32[]{:S(2)}) collective-permute-start(f32[3,1,18,128]{2,1,3,0:T(1,128)S(1)} %get-tuple-element.34), channel_id=1, source_target_pairs={{0,4},{4,8},{8,12},{12,16},{16,20},{20,24},{24,28},{28,0},{1,5},{5... | collective-permute-start | bytes 82952 | tf_op jit(solution)/shard_map/ppermute | solution.py:18
  163.9 1.7 copy-start.11
  171.9 49.4 %copy-start.1 = (f32[64]{0:T(128)S(1)}, f32[64]{0:T(128)}, u32[]{:S(2)}) copy-start(f32[64]{0:T(128)} %param.13) | copy-start | bytes 772
where the time goes:
time: 223 us; the launch traced here: 222 us
  blocking collectives  85 us (38%)
  other arithmetic  66.1 us (30%)
  local copies, waits for them, and re-layouts  29.3 us (13%)
  starting transfers between devices  22.2 us (10%)
  waiting for transfers between devices  15.7 us (7%)
  between operations  3.04 us (1%)
    psum x1, blocking collectives, shards(): total_sq = lax.psum(square_sum, ('az', 'ax'))  43 us
    psum x1, blocking collectives, shards(): liner_grad = lax.psum(segment_sums, ('az', 'ax')) * grad_scale  41.9 us
    slice x2, other arithmetic, with_halo(): last = lax.slice_in_dim(array, length - width, length, axis=dim)  16.5 us
    ppermute x6, starting transfers between devices, with_halo(): before = lax.ppermute(last, axis, up)  13.2 us
    another operation x4, other arithmetic, second_half(): jnp.stack([back_press, back_az, back_ax, back_rad])  10.7 us
    concatenate x3, other arithmetic, with_halo(): array = jnp.concatenate([before, array, after], axis=dim)  9.38 us
    ppermute x6, starting transfers between devices, with_halo(): after = lax.ppermute(initial, axis, down)  8.97 us
    ppermute x6, waiting for transfers between devices, with_halo(): before = lax.ppermute(last, axis, up)  8.08 us
  transfers between devices with their start and end apart: 12, of which 7 were waited for; matrix products, arithmetic and copies ran while one was open for 7% of the time, Pallas kernels for 0%

commit v1 on v0

--- a/solution.py
+++ b/solution.py
@@ -216,7 +216,7 @@
     outcome = adjoint_step([seed_press], [velocities], coef_wide, wall_admit, rim_width)
     adjoint_out, rad_top = outcome[0]
     segment_sums = jnp.einsum("acs,ac->s", segment_hot, rad_top * casing_own, precision=highest)
-    liner_grad = lax.psum(segment_sums, ("az", "ax")) * grad_scale
+    liner_grad = lax.psum(lax.psum(segment_sums, "ax"), "az") * grad_scale
     misfit = 0.5 * jnp.log(mean_sq)
     return (adjoint_out, liner_grad, misfit)
 

time: 223 us -> 211 us (0.946)
  the two profiles are of different devices: /device:TPU:14 before, /device:TPU:0 now
where the time goes in v1:
time: 211 us; the launch traced here: 210 us
  other arithmetic  66.1 us (31%)
  blocking collectives  64 us (30%)
  local copies, waits for them, and re-layouts  29.3 us (14%)
  starting transfers between devices  25.7 us (12%)
  waiting for transfers between devices  20.7 us (10%)
  between operations  3.07 us (1%)
    psum x1, blocking collectives, shards(): total_sq = lax.psum(square_sum, ('az', 'ax'))  37.3 us
    psum x2, blocking collectives, shards(): liner_grad = lax.psum(lax.psum(segment_sums, 'ax'), 'az') * grad_scale  26.8 us
    slice x2, other arithmetic, with_halo(): last = lax.slice_in_dim(array, length - width, length, axis=dim)  16.5 us
    ppermute x6, starting transfers between devices, with_halo(): after = lax.ppermute(initial, axis, down)  14.6 us
    ppermute x6, waiting for transfers between devices, with_halo(): before = lax.ppermute(last, axis, up)  14.2 us
    ppermute x6, starting transfers between devices, with_halo(): before = lax.ppermute(last, axis, up)  11.1 us
    another operation x4, other arithmetic, second_half(): jnp.stack([back_press, back_az, back_ax, back_rad])  10.7 us
    concatenate x3, other arithmetic, with_halo(): array = jnp.concatenate([before, array, after], axis=dim)  9.38 us
  transfers between devices with their start and end apart: 12, of which 6 were waited for; matrix products, arithmetic and copies ran while one was open for 7% of the time, Pallas kernels for 0%

profile of v1, /device:TPU:0, one launch (start us, length us, event | category | flops | bytes accessed | tf_op | source)
XLA Modules:
  0.0 210.0 jit_solution(2860851315141875054)
XLA Ops:
  0.6 0.9 slice_divide_fusion
  1.5 0.9 slice.363
  2.5 1.0 pad_maximum_fusion.6
  3.7 1.3 collective-permute-start.1
  5.0 3.0 %collective-permute-start = (f32[8,8,2,128]{3,1,2,0:T(8,128)S(1)}, f32[8,8,2,128]{3,1,2,0:T(8,128)S(1)}, u32[]{:S(2)}, u32[]{:S(2)}) collective-permute-start(f32[8,8,2,128]{3,1,2,0:T(8,128)S(1)} %copy.107), channel_id=1, source_target_pairs={{0,1},{1,2},{2,3},{4,5},{5,6},{6,7},{8,9},{9,10},{10,11},{12,13},{... | collective-permute-start | bytes 196616 | tf_op jit(solution)/shard_map/ppermute | solution.py:18
  8.0 2.7 %copy.81 = f32[8,8,16,128]{2,1,3,0:T(8,128)} copy(f32[8,8,16,128]{3,2,1,0:T(8,128)S(1)} %pad_maximum_fusion.6) | data formatting | bytes 1048576 | tf_op jit(solution)/shard_map/concatenate | solution.py:189
  11.6 2.7 %copy.82 = f32[8,8,2,128]{2,1,3,0:T(8,128)} copy(f32[8,8,2,128]{3,1,2,0:T(8,128)S(1)} %collective-permute-done.1) | data formatting | bytes 131072 | tf_op jit(solution)/shard_map/ppermute | solution.py:19
  14.3 2.7 %copy.80 = f32[8,8,2,128]{2,1,3,0:T(8,128)} copy(f32[8,8,2,128]{3,1,2,0:T(8,128)S(1)} %collective-permute-done) | data formatting | bytes 131072 | tf_op jit(solution)/shard_map/ppermute | solution.py:18
  17.0 12.7 %pad_maximum_fusion.5 = (f32[8,2,20,128]{2,1,3,0:T(2,128)S(1)}, f32[8,2,20,128]{2,1,3,0:T(2,128)S(1)}) fusion(f32[8,8,2,128]{2,1,3,0:T(8,128)} %copy.82, f32[8,8,16,128]{2,1,3,0:T(8,128)} %copy.81, f32[8,8,2,128]{2,1,3,0:T(8,128)} %copy.80), kind=kLoop, calls=%fused_computation.47 | loop fusion | flops 163840 | bytes 983040 | tf_op jit(solution)/shard_map/slice | solution.py:16
  30.0 6.1 %collective-permute-start.3 = (f32[8,2,20,128]{3,0,2,1:T(8,128)S(1)}, f32[8,2,20,128]{3,0,2,1:T(8,128)S(1)}, u32[]{:S(2)}, u32[]{:S(2)}) collective-permute-start(f32[8,2,20,128]{3,0,2,1:T(8,128)S(1)} %copy.84), channel_id=1, source_target_pairs={{4,0},{8,4},{12,8},{16,12},{20,16},{24,20},{28,24},{0,28},{5,1},{9... | collective-permute-start | bytes 491528 | tf_op jit(solution)/shard_map/ppermute | solution.py:19
  37.3 3.2 %collective-permute-done.3 = f32[8,2,20,128]{3,0,2,1:T(8,128)S(1)} collective-permute-done((f32[8,2,20,128]{3,0,2,1:T(8,128)S(1)}, f32[8,2,20,128]{3,0,2,1:T(8,128)S(1)}, u32[]{:S(2)}, u32[]{:S(2)}) %collective-permute-start.3) | collective-permute-done | bytes 163872 | tf_op jit(solution)/shard_map/ppermute | solution.py:19
  41.0 5.3 %collective-permute-done.2 = f32[8,2,20,128]{3,0,2,1:T(8,128)S(1)} collective-permute-done((f32[8,2,20,128]{3,0,2,1:T(8,128)S(1)}, f32[8,2,20,128]{3,0,2,1:T(8,128)S(1)}, u32[]{:S(2)}, u32[]{:S(2)}) %collective-permute-start.2) | collective-permute-done | bytes 163872 | tf_op jit(solution)/shard_map/ppermute | solution.py:18
  46.8 7.7 %pad_maximum_fusion = f32[8,12,20,128]{2,1,3,0:T(8,128)S(1)} fusion(f32[8,2,20,128]{2,1,3,0:T(2,128)S(1)} %copy.86, f32[8,8,2,128]{2,1,3,0:T(8,128)} %copy.82, f32[8,8,16,128]{2,1,3,0:T(8,128)} %copy.81, f32[8,8,2,128]{2,1,3,0:T(8,128)} %copy.80, f32[8,2,20,128]{2,1,3,0:T(2,128)S(1)} %copy.85), kind=kLoop, calls=%fused_computation.2 | loop fusion | flops 983040 | bytes 1966080 | tf_op jit(solution)/shard_map/concatenate | solution.py:20
  55.0 2.7 %copy-done.2 = f32[8,12,20,128]{2,1,3,0:T(8,128)} copy-done((f32[8,12,20,128]{2,1,3,0:T(8,128)}, f32[8,12,20,128]{2,1,3,0:T(8,128)S(1)}, u32[]{:S(2)}) %copy-start.2) | copy-done | bytes 983064
  58.1 2.5 %fusion.5 = f32[10,18,128]{1,0,2:T(8,128)S(1)} fusion(f32[12,20,128]{1,0,2:T(8,128)S(1)} %get-tuple-element.33, f32[12,20,128]{1,0,2:T(8,128)S(1)} %get-tuple-element.28, f32[12,20,128]{1,0,2:T(8,128)S(1)} %get-tuple-element.29, f32[12,20,128]{1,0,2:T(8,128)S(1)} %get-tuple-element.31, f32[12,20,128]{1,0,2:T(8,128)S(1)} %get-tuple-element.32), kind=kLoop, calls=%fused_computation.20 | loop fusion | flops 253440 | bytes 1013760 | tf_op jit(solution)/shard_map/sub | solution.py:87
  60.6 2.5 %fusion.13 = f32[10,18,128]{1,0,2:T(8,128)S(1)} fusion(f32[12,20,128]{1,0,2:T(8,128)S(1)} %get-tuple-element.33, f32[12,20,128]{1,0,2:T(8,128)S(1)} %get-tuple-element.26, f32[12,20,128]{1,0,2:T(8,128)S(1)} %get-tuple-element.29, f32[12,20,128]{1,0,2:T(8,128)S(1)} %get-tuple-element.31, f32[12,20,128]{1,0,2:T(8,128)S(1)} %get-tuple-element.32), kind=kLoop, calls=%fused_computation.32 | loop fusion | flops 253440 | bytes 1013760 | tf_op jit(solution)/shard_map/sub | solution.py:83
  63.1 2.0 fusion.62
  65.6 0.7 fusion.69
  66.4 3.3 %gather_fusion = f32[512]{0:T(512)S(1)} fusion(f32[128]{0:T(128)S(1)} %reshape_squeeze.3, s32[1024]{0:T(1024)S(1)} %pad_clamp_fusion), kind=kCustom, calls=%fused_computation | custom fusion | bytes 6144 | tf_op jit(solution)/shard_map/gather | solution.py:199
  70.4 37.3 %psum.21 = f32[]{:T(128)} all-reduce(f32[]{:T(128)} %get-tuple-element.11), channel_id=1, replica_groups=mesh['az'=8,'ax'=4] {'az','ax'}, use_global_device_ids=true, to_apply=%region_1.2 | all-reduce | flops 1 | bytes 8 | tf_op jit(solution)/shard_map/psum | solution.py:207
  108.3 4.1 %scatter_custom_fusion = f32[128]{0:T(128)S(1)} fusion(s32[512]{0:T(512)S(1)} %compare_select_fusion, f32[512]{0:T(512)S(1)} %divide_select_fusion, f32[]{:T(128)} %constant.19.clone.1), kind=kCustom, calls=%fused_computation.159 | custom fusion | flops 512 | bytes 516 | tf_op jit(solution)/shard_map/scatter-add | solution.py:212
  112.7 1.3 collective-permute-start.5
  114.0 3.0 %collective-permute-start.4 = (f32[1,8,1,128]{3,1,2,0:T(8,128)S(1)}, f32[1,8,1,128]{3,1,2,0:T(8,128)S(1)}, u32[]{:S(2)}, u32[]{:S(2)}) collective-permute-start(f32[1,8,1,128]{3,1,2,0:T(8,128)S(1)} %get-tuple-element.60), channel_id=1, source_target_pairs={{0,1},{1,2},{2,3},{4,5},{5,6},{6,7},{8,9},{9,10},{10,11},{12,13},{... | collective-permute-start | bytes 12296 | tf_op jit(solution)/shard_map/ppermute | solution.py:18
  117.0 0.8 collective-permute-done.4
  118.0 4.3 %collective-permute-start.7 = (f32[1,1,18,128]{2,1,3,0:T(1,128)S(1)}, f32[1,1,18,128]{2,1,3,0:T(1,128)S(1)}, u32[]{:S(2)}, u32[]{:S(2)}) collective-permute-start(f32[1,1,18,128]{2,1,3,0:T(1,128)S(1)} %copy.89), channel_id=1, source_target_pairs={{4,0},{8,4},{12,8},{16,12},{20,16},{24,20},{28,24},{0,28},{5,1},{9... | collective-permute-start | bytes 27656 | tf_op jit(solution)/shard_map/ppermute | solution.py:19
  123.1 1.0 copy.112
  124.4 4.9 %collective-permute-done.6 = f32[1,1,18,128]{2,1,3,0:T(1,128)S(1)} collective-permute-done((f32[1,1,18,128]{2,1,3,0:T(1,128)S(1)}, f32[1,1,18,128]{2,1,3,0:T(1,128)S(1)}, u32[]{:S(2)}, u32[]{:S(2)}) %collective-permute-start.6) | collective-permute-done | bytes 9248 | tf_op jit(solution)/shard_map/ppermute | solution.py:18
  129.3 4.1 %fusion.21 = (f32[10,18,128]{1,0,2:T(8,128)}, f32[10,18,128]{1,0,2:T(8,128)S(1)}, f32[10,18,128]{1,0,2:T(8,128)}) fusion(f32[8,12,20,128]{2,1,3,0:T(8,128)} %copy-done.2, f32[1,1,18,128]{2,1,3,0:T(1,128)S(1)} %collective-permute-done.7, f32[1,8,18,128]{2,1,3,0:T(8,128)S(1)} %copy.90, f32[1,1,18,128]{2,1,3,0:T(1,128)S(1)} %collective-permute-done.6), kind=kLoop, calls=%fused_computation.54 | loop fusion | flops 138240 | bytes 645120 | tf_op jit(solution)/shard_map/mul | solution.py:68
  135.9 1.3 collective-permute-start.9
  137.7 3.0 %collective-permute-start.8 = (f32[3,8,1,128]{3,1,2,0:T(8,128)S(1)}, f32[3,8,1,128]{3,1,2,0:T(8,128)S(1)}, u32[]{:S(2)}, u32[]{:S(2)}) collective-permute-start(f32[3,8,1,128]{3,1,2,0:T(8,128)S(1)} %copy.94), channel_id=1, source_target_pairs={{0,1},{1,2},{2,3},{4,5},{5,6},{6,7},{8,9},{9,10},{10,11},{12,13},{... | collective-permute-start | bytes 36872 | tf_op jit(solution)/shard_map/ppermute | solution.py:18
  140.7 2.6 %slice_bitcast_fusion.3 = f32[10,18,128]{1,0,2:T(8,128)} fusion(f32[8,12,20,128]{2,1,3,0:T(8,128)} %copy-done.2), kind=kLoop, calls=%fused_computation.12 | loop fusion | bytes 184320 | tf_op jit(solution)/shard_map/squeeze | solution.py:130
  144.5 3.8 %pad_maximum_fusion.12 = (f32[3,1,18,128]{2,1,3,0:T(1,128)S(1)}, f32[3,1,18,128]{2,1,3,0:T(1,128)S(1)}) fusion(f32[3,8,1,128]{2,1,3,0:T(8,128)S(1)} %copy.97, f32[3,8,1,128]{2,1,3,0:T(8,128)S(1)} %copy.96, f32[1,8,16,128]{2,1,3,0:T(8,128)} %copy-done.7, f32[1,8,16,128]{2,1,3,0:T(8,128)} %copy-done.5, f32[1,8,16,128]{2,1,3,0:T(8,128)} %copy-done.3), kind=kLoop, calls=%fused_computation.127 | loop fusion | flops 55296 | bytes 276480 | tf_op jit(solution)/shard_map/slice | solution.py:16
  148.7 1.7 collective-permute-start.10
  150.4 1.2 maximum_bitcast_fusion
  151.7 3.3 %collective-permute-done.11 = f32[3,1,18,128]{2,1,3,0:T(1,128)S(1)} collective-permute-done((f32[3,1,18,128]{2,1,3,0:T(1,128)S(1)}, f32[3,1,18,128]{2,1,3,0:T(1,128)S(1)}, u32[]{:S(2)}, u32[]{:S(2)}) %collective-permute-start.11) | collective-permute-done | bytes 27680 | tf_op jit(solution)/shard_map/ppermute | solution.py:19
  155.0 3.1 %collective-permute-done.10 = f32[3,1,18,128]{2,1,3,0:T(1,128)S(1)} collective-permute-done((f32[3,1,18,128]{2,1,3,0:T(1,128)S(1)}, f32[3,1,18,128]{2,1,3,0:T(1,128)S(1)}, u32[]{:S(2)}, u32[]{:S(2)}) %collective-permute-start.10) | collective-permute-done | bytes 27680 | tf_op jit(solution)/shard_map/ppermute | solution.py:18
  158.1 1.7 pad_maximum_fusion.1
  159.9 4.9 %multiply_multiply_fusion.1 = (f32[10,18,128]{1,0,2:T(8,128)}, f32[10,18,128]{1,0,2:T(8,128)}, f32[10,18,128]{1,0,2:T(8,128)S(1)}, f32[10,18,128]{1,0,2:T(8,128)...) fusion(f32[8,12,20,128]{2,1,3,0:T(8,128)} %copy-done.2, ...), kind=kLoop, calls=%fused_computation.50 | loop fusion | flops 207360 | bytes 1290368 | tf_op jit(solution)/shard_map/mul | solution.py:136
  164.8 1.8 slice_bitcast_fusion
  166.6 1.7 fusion.22
  168.2 0.7 fusion.41
  169.2 3.1 %fusion.33 = f32[1,8,16,128]{2,1,3,0:T(8,128)S(1)} fusion(f32[10,18,128]{1,0,2:T(8,128)} %get-tuple-element.18, f32[10,18,128]{1,0,2:T(8,128)} %get-tuple-element.20, f32[10,18,128]{1,0,2:T(8,128)} %get-tuple-element.37), kind=kLoop, calls=%fused_computation.69 | loop fusion | flops 81920 | bytes 393216 | tf_op jit(solution)/shard_map/stack | solution.py:148
  172.5 1.9 fusion.37
  174.6 5.0 %fusion.40 = f32[1,8,16,128]{2,1,3,0:T(8,128)S(1)} fusion(f32[10,18,128]{1,0,2:T(8,128)} %get-tuple-element.36, f32[10,18,128]{1,0,2:T(8,128)} %get-tuple-element.16, f32[10,18,128]{1,0,2:T(8,128)} %get-tuple-element.15, f32[10,18,128]{1,0,2:T(8,128)} %get-tuple-element.25, f32[10,18,128]{1,0,2:T(8,128)} %get-tuple-element.23, ...), kind=kLoop, calls=%fused_computation.80 | loop fusion | flops 229376 | bytes 852096 | tf_op jit(solution)/shard_map/stack | solution.py:148
  179.8 0.8 slice_multiply_fusion.4
  180.8 7.8 %psum.22 = f32[64]{0:T(128)S(1)} all-reduce(f32[64]{0:T(128)S(1)} %convolution_bitcast_fusion), channel_id=1, replica_groups=mesh['az'=8,'ax'=4] {'ax'}, use_global_device_ids=true, to_apply=%region_3.4 | all-reduce | flops 64 | bytes 512 | tf_op jit(solution)/shard_map/psum | solution.py:219
  188.6 19.0 %psum.23 = f32[64]{0:T(128)S(1)} all-reduce(f32[64]{0:T(128)S(1)} %psum.22), channel_id=1, replica_groups=mesh['az'=8,'ax'=4] {'az'}, use_global_device_ids=true, to_apply=%region_4.5 | all-reduce | flops 64 | bytes 512 | tf_op jit(solution)/shard_map/psum | solution.py:219
  208.1 0.7 pad_maximum_fusion.7
  (98 shorter events, 13.1 us)
Async XLA Ops:
  0.6 10.1 %copy-start = (f32[64]{0:T(128)S(1)}, f32[64]{0:T(128)}, u32[]{:S(2)}) copy-start(f32[64]{0:T(128)} %param.13) | copy-start | bytes 772
  2.5 8.2 %copy-start.12 = (f32[4,8,16,128]{3,2,1,0:T(8,128)S(1)}, f32[4,8,16,128]{3,2,1,0:T(8,128)}, u32[]{:S(2)}) copy-start(f32[4,8,16,128]{3,2,1,0:T(8,128)} %param.12) | copy-start | bytes 786436
  3.5 7.2 %copy-start.17 = (s32[8,16]{1,0:T(8,128)S(1)}, s32[8,16]{1,0:T(8,128)}, u32[]{:S(2)}) copy-start(s32[8,16]{1,0:T(8,128)} %param.14) | copy-start | bytes 1540
  3.5 7.6 %copy-start.16 = (s32[8,16]{1,0:T(8,128)S(1)}, s32[8,16]{1,0:T(8,128)}, u32[]{:S(2)}) copy-start(s32[8,16]{1,0:T(8,128)} %param.15) | copy-start | bytes 1540
  3.5 7.6 %copy-start.18 = (f32[64]{0:T(128)S(1)}, f32[64]{0:T(128)}, u32[]{:S(2)}) copy-start(f32[64]{0:T(128)} %param.16) | copy-start | bytes 772
  3.6 8.0 %copy-start.13 = (s32[512]{0:T(512)S(1)}, s32[512]{0:T(512)}, u32[]{:S(2)}) copy-start(s32[512]{0:T(512)} %param.18) | copy-start | bytes 6148
  3.6 8.0 %copy-start.14 = (s32[512]{0:T(512)S(1)}, s32[512]{0:T(512)}, u32[]{:S(2)}) copy-start(s32[512]{0:T(512)} %param.17) | copy-start | bytes 6148
  3.7 8.0 %collective-permute-start.1 = (f32[8,8,2,128]{3,1,2,0:T(8,128)S(1)}, f32[8,8,2,128]{3,1,2,0:T(8,128)S(1)}, u32[]{:S(2)}, u32[]{:S(2)}) collective-permute-start(f32[8,8,2,128]{3,1,2,0:T(8,128)S(1)} %copy.108), channel_id=1, source_target_pairs={{1,0},{2,1},{3,2},{5,4},{6,5},{7,6},{9,8},{10,9},{11,10},{13,12},{... | collective-permute-start | bytes 196616 | tf_op jit(solution)/shard_map/ppermute | solution.py:19
  5.0 9.3 %collective-permute-start = (f32[8,8,2,128]{3,1,2,0:T(8,128)S(1)}, f32[8,8,2,128]{3,1,2,0:T(8,128)S(1)}, u32[]{:S(2)}, u32[]{:S(2)}) collective-permute-start(f32[8,8,2,128]{3,1,2,0:T(8,128)S(1)} %copy.107), channel_id=1, source_target_pairs={{0,1},{1,2},{2,3},{4,5},{5,6},{6,7},{8,9},{9,10},{10,11},{12,13},{... | collective-permute-start | bytes 196616 | tf_op jit(solution)/shard_map/ppermute | solution.py:18
  30.0 10.5 %collective-permute-start.3 = (f32[8,2,20,128]{3,0,2,1:T(8,128)S(1)}, f32[8,2,20,128]{3,0,2,1:T(8,128)S(1)}, u32[]{:S(2)}, u32[]{:S(2)}) collective-permute-start(f32[8,2,20,128]{3,0,2,1:T(8,128)S(1)} %copy.84), channel_id=1, source_target_pairs={{4,0},{8,4},{12,8},{16,12},{20,16},{24,20},{28,24},{0,28},{5,1},{9... | collective-permute-start | bytes 491528 | tf_op jit(solution)/shard_map/ppermute | solution.py:19
  36.5 9.9 %collective-permute-start.2 = (f32[8,2,20,128]{3,0,2,1:T(8,128)S(1)}, f32[8,2,20,128]{3,0,2,1:T(8,128)S(1)}, u32[]{:S(2)}, u32[]{:S(2)}) collective-permute-start(f32[8,2,20,128]{3,0,2,1:T(8,128)S(1)} %copy.83), channel_id=1, source_target_pairs={{0,4},{4,8},{8,12},{12,16},{16,20},{20,24},{24,28},{28,0},{1,5},{5... | collective-permute-start | bytes 491528 | tf_op jit(solution)/shard_map/ppermute | solution.py:18
  54.5 3.3 %copy-start.2 = (f32[8,12,20,128]{2,1,3,0:T(8,128)}, f32[8,12,20,128]{2,1,3,0:T(8,128)S(1)}, u32[]{:S(2)}) copy-start(f32[8,12,20,128]{2,1,3,0:T(8,128)S(1)} %pad_maximum_fusion) | copy-start | bytes 2949124
  65.1 4.6 %copy-start.15 = (f32[512]{0:T(512)S(1)}, f32[512]{0:T(512)}, u32[]{:S(2)}) copy-start(f32[512]{0:T(512)} %param.19) | copy-start | bytes 6148
  65.6 57.5 %slice-start = ((f32[4,8,16,128]{3,2,1,0:T(8,128)}), f32[1,8,16,128]{3,2,1,0:T(8,128)S(1)}, s32[]{:S(2)}) async-start(f32[4,8,16,128]{3,2,1,0:T(8,128)} %param.10), calls=%async_computation | async-start | bytes 131072 | tf_op jit(solution)/shard_map/slice | solution.py:203
  112.7 4.3 %collective-permute-start.5 = (f32[1,8,1,128]{3,1,2,0:T(8,128)S(1)}, f32[1,8,1,128]{3,1,2,0:T(8,128)S(1)}, u32[]{:S(2)}, u32[]{:S(2)}) collective-permute-start(f32[1,8,1,128]{3,1,2,0:T(8,128)S(1)} %get-tuple-element.61), channel_id=1, source_target_pairs={{1,0},{2,1},{3,2},{5,4},{6,5},{7,6},{9,8},{10,9},{11,10},{13,12},{... | collective-permute-start | bytes 12296 | tf_op jit(solution)/shard_map/ppermute | solution.py:19
  114.0 3.8 %collective-permute-start.4 = (f32[1,8,1,128]{3,1,2,0:T(8,128)S(1)}, f32[1,8,1,128]{3,1,2,0:T(8,128)S(1)}, u32[]{:S(2)}, u32[]{:S(2)}) collective-permute-start(f32[1,8,1,128]{3,1,2,0:T(8,128)S(1)} %get-tuple-element.60), channel_id=1, source_target_pairs={{0,1},{1,2},{2,3},{4,5},{5,6},{6,7},{8,9},{9,10},{10,11},{12,13},{... | collective-permute-start | bytes 12296 | tf_op jit(solution)/shard_map/ppermute | solution.py:18
  118.0 6.4 %collective-permute-start.7 = (f32[1,1,18,128]{2,1,3,0:T(1,128)S(1)}, f32[1,1,18,128]{2,1,3,0:T(1,128)S(1)}, u32[]{:S(2)}, u32[]{:S(2)}) collective-permute-start(f32[1,1,18,128]{2,1,3,0:T(1,128)S(1)} %copy.89), channel_id=1, source_target_pairs={{4,0},{8,4},{12,8},{16,12},{20,16},{24,20},{28,24},{0,28},{5,1},{9... | collective-permute-start | bytes 27656 | tf_op jit(solution)/shard_map/ppermute | solution.py:19
  122.3 7.0 %collective-permute-start.6 = (f32[1,1,18,128]{2,1,3,0:T(1,128)S(1)}, f32[1,1,18,128]{2,1,3,0:T(1,128)S(1)}, u32[]{:S(2)}, u32[]{:S(2)}) collective-permute-start(f32[1,1,18,128]{2,1,3,0:T(1,128)S(1)} %copy.88), channel_id=1, source_target_pairs={{0,4},{4,8},{8,12},{12,16},{16,20},{20,24},{24,28},{28,0},{1,5},{5... | collective-permute-start | bytes 27656 | tf_op jit(solution)/shard_map/ppermute | solution.py:18
  124.4 9.1 %copy-start.9 = (f32[1,8,18,128]{2,1,3,0:T(8,128)}, f32[1,8,18,128]{2,1,3,0:T(8,128)S(1)}, u32[]{:S(2)}) copy-start(f32[1,8,18,128]{2,1,3,0:T(8,128)S(1)} %copy.90) | copy-start | bytes 221188
  134.2 0.8 copy-start.3
  134.2 1.0 copy-start.5
  134.2 1.1 copy-start.7
  135.9 7.5 %collective-permute-start.9 = (f32[3,8,1,128]{3,1,2,0:T(8,128)S(1)}, f32[3,8,1,128]{3,1,2,0:T(8,128)S(1)}, u32[]{:S(2)}, u32[]{:S(2)}) collective-permute-start(f32[3,8,1,128]{3,1,2,0:T(8,128)S(1)} %copy.95), channel_id=1, source_target_pairs={{1,0},{2,1},{3,2},{5,4},{6,5},{7,6},{9,8},{10,9},{11,10},{13,12},{... | collective-permute-start | bytes 36872 | tf_op jit(solution)/shard_map/ppermute | solution.py:19
  137.7 6.3 %collective-permute-start.8 = (f32[3,8,1,128]{3,1,2,0:T(8,128)S(1)}, f32[3,8,1,128]{3,1,2,0:T(8,128)S(1)}, u32[]{:S(2)}, u32[]{:S(2)}) collective-permute-start(f32[3,8,1,128]{3,1,2,0:T(8,128)S(1)} %copy.94), channel_id=1, source_target_pairs={{0,1},{1,2},{2,3},{4,5},{5,6},{6,7},{8,9},{9,10},{10,11},{12,13},{... | collective-permute-start | bytes 36872 | tf_op jit(solution)/shard_map/ppermute | solution.py:18
  144.5 5.9 %copy-start.10 = (f32[1,8,18,128]{2,1,3,0:T(8,128)S(1)}, f32[1,8,18,128]{2,1,3,0:T(8,128)}, u32[]{:S(2)}) copy-start(f32[1,8,18,128]{2,1,3,0:T(8,128)} %copy-done.9) | copy-start | bytes 221188
  144.5 13.6 %copy-start.4 = (f32[1,8,16,128]{2,1,3,0:T(8,128)S(1)}, f32[1,8,16,128]{2,1,3,0:T(8,128)}, u32[]{:S(2)}) copy-start(f32[1,8,16,128]{2,1,3,0:T(8,128)} %copy-done.3) | copy-start | bytes 196612
  144.5 13.6 %copy-start.6 = (f32[1,8,16,128]{2,1,3,0:T(8,128)S(1)}, f32[1,8,16,128]{2,1,3,0:T(8,128)}, u32[]{:S(2)}) copy-start(f32[1,8,16,128]{2,1,3,0:T(8,128)} %copy-done.5) | copy-start | bytes 196612
  144.5 13.6 %copy-start.8 = (f32[1,8,16,128]{2,1,3,0:T(8,128)S(1)}, f32[1,8,16,128]{2,1,3,0:T(8,128)}, u32[]{:S(2)}) copy-start(f32[1,8,16,128]{2,1,3,0:T(8,128)} %copy-done.7) | copy-start | bytes 196612
  148.4 6.6 %collective-permute-start.11 = (f32[3,1,18,128]{2,1,3,0:T(1,128)S(1)}, f32[3,1,18,128]{2,1,3,0:T(1,128)S(1)}, u32[]{:S(2)}, u32[]{:S(2)}) collective-permute-start(f32[3,1,18,128]{2,1,3,0:T(1,128)S(1)} %get-tuple-element.35), channel_id=1, source_target_pairs={{4,0},{8,4},{12,8},{16,12},{20,16},{24,20},{28,24},{0,28},{5,1},{9... | collective-permute-start | bytes 82952 | tf_op jit(solution)/shard_map/ppermute | solution.py:19
  148.7 9.4 %collective-permute-start.10 = (f32[3,1,18,128]{2,1,3,0:T(1,128)S(1)}, f32[3,1,18,128]{2,1,3,0:T(1,128)S(1)}, u32[]{:S(2)}, u32[]{:S(2)}) collective-permute-start(f32[3,1,18,128]{2,1,3,0:T(1,128)S(1)} %get-tuple-element.34), channel_id=1, source_target_pairs={{0,4},{4,8},{8,12},{12,16},{16,20},{20,24},{24,28},{28,0},{1,5},{5... | collective-permute-start | bytes 82952 | tf_op jit(solution)/shard_map/ppermute | solution.py:18
  166.5 1.7 copy-start.11
  174.6 34.2 %copy-start.1 = (f32[64]{0:T(128)S(1)}, f32[64]{0:T(128)}, u32[]{:S(2)}) copy-start(f32[64]{0:T(128)} %param.13) | copy-start | bytes 772
